TPU v7x, 32 devices: a whole 2x2x4 slice. The times are simulated.
32 devices in a mesh: gx: 4 (over x, core), gy: 8 (over z, y).
Axes of the slice: x: 2, y: 2, z: 4, core: 2. Of those that a mesh axis runs over, the one named last changes fastest.
Arguments:
- right_side: float32 [4, 1024, 2048], P(None, 'gx', 'gy')
- prior_weight: float32 [4, 1024, 2048], P(None, 'gx', 'gy'), may hold values from 0.5 to 4
- jacobi_inverse: float32 [4, 1024, 2048], P(None, 'gx', 'gy'), may hold values from 0.1 to 0.5
- interaction: float32 [2, 4, 128, 128], replicated, may hold values from -0.5 to 0.5
- footprint: int32 [2, 16, 16, 4], P(None, 'gx', 'gy'), may hold values from 0 to 255, as said below
Outputs:
- solution: float32 [4, 1024, 2048], P(None, 'gx', 'gy')
- residual: float32 [4, 1024, 2048], P(None, 'gx', 'gy')
Inputs may be any that keep to these rules, and one draw needn't show every extreme that they name: `footprint`: each entry is bx * 16 + by of a block of the same 4 block rows along the first dimension as its ray block's tile. Of the 64 entries of one tile's ray blocks, between 7 and 9 fall in each tile of the same strip along the second dimension, exactly 9 in some; one tile of the second dimension receives exactly 9 entries from every tile of the strip.
All inputs are finite; a program needn't handle non-finite values.
Results may differ from a plain program's by a relative error of at most 0.0003.
Values sent between devices are 32-bit elements; how exact they have to be, the bound alone decides.
No kernel may reach another device: no remote copies, remote signals or barrier semaphores. Data moves between devices by JAX's collectives and lax.ppermute only.
A program may use at most 128 MiB of HBM per device.

v0:
```python
import jax
import jax.numpy as jnp
from jax import lax
from jax.sharding import PartitionSpec as P

ITERS = 4
DAUB_LOW = (
    0.3326705529509569,
    0.8068915093133388,
    0.4598775021193313,
    -0.13501102001039084,
    -0.08544127388224149,
    0.035226291882100656,
)
DAUB_HIGH = tuple(((-1.0) ** tap_index * DAUB_LOW[5 - tap_index] for tap_index in range(6)))


def extended(block, sides, width):
    for axis, dim in sides:
        count = lax.axis_size(axis)
        forward = [(i, i + 1) for i in range(count - 1)]
        backward = [(target, source) for source, target in forward]
        low = lax.ppermute(
            lax.slice_in_dim(block, block.shape[dim] - width, None, axis=dim), axis, forward
        )
        high = lax.ppermute(lax.slice_in_dim(block, 0, width, axis=dim), axis, backward)
        block = jnp.concatenate([low, block, high], axis=dim)
    return block


def synth_table(length):
    inputs = jnp.arange(length + 8, dtype=jnp.int32)[:, None]
    outputs = jnp.arange(length, dtype=jnp.int32)[None, :]
    half = outputs // 2
    phase = outputs % 2
    table = jnp.zeros((length + 8, length), jnp.float32)
    for tap_num in range(3):
        low_coef = jnp.where(phase == 0, DAUB_LOW[2 * tap_num], DAUB_LOW[2 * tap_num + 1])
        high_coef = jnp.where(phase == 0, DAUB_HIGH[2 * tap_num], DAUB_HIGH[2 * tap_num + 1])
        table = table + jnp.where(inputs == 2 * (half - tap_num) + 4, low_coef, 0.0)
        table = table + jnp.where(inputs == 2 * (half - tap_num) + 5, high_coef, 0.0)
    return table


def analysis_table(length):
    inputs = jnp.arange(length + 8, dtype=jnp.int32)[:, None]
    outputs = jnp.arange(length, dtype=jnp.int32)[None, :]
    half = outputs // 2
    phase = outputs % 2
    table = jnp.zeros((length + 8, length), jnp.float32)
    for tap_num in range(3):
        for offset in (0, 1):
            coef = jnp.where(
                phase == 0, DAUB_LOW[2 * tap_num + offset], DAUB_HIGH[2 * tap_num + offset]
            )
            table = table + jnp.where(inputs == 2 * (half + tap_num) + offset + 4, coef, 0.0)
    return table


def with_rim(field):
    return extended(field, (("gx", 1), ("gy", 2)), 4)


def shards(right_side, prior_weight, jacobi_inverse, interaction, footprint):
    highest = lax.Precision.HIGHEST
    layers, tile_rows, tile_cols = right_side.shape
    sensors, rows_blocks, cols_blocks = (footprint.shape[0], footprint.shape[1], footprint.shape[2])
    block_rows = tile_rows // rows_blocks
    block_cols = tile_cols // cols_blocks
    owners = lax.axis_size("gy")
    layer_blocks_cols = cols_blocks * owners
    requests = sensors * rows_blocks * cols_blocks * layers
    capacity = requests // owners + 1
    own_blocks = layers * rows_blocks * cols_blocks
    synth_rows = synth_table(tile_rows)
    synth_cols = synth_table(tile_cols)
    analysis_rows = analysis_table(tile_rows)
    analysis_cols = analysis_table(tile_cols)
    flat_ids = footprint.reshape(requests)
    request_num = jnp.arange(requests, dtype=jnp.int32)
    layer_of = request_num % layers
    sensor_of = request_num // (requests // sensors)
    target = flat_ids % layer_blocks_cols // cols_blocks
    owned_index = (
        layer_of * (rows_blocks * cols_blocks)
        + flat_ids // layer_blocks_cols % rows_blocks * cols_blocks
        + flat_ids % layer_blocks_cols % cols_blocks
    )
    picks = (target[:, None] == jnp.arange(owners, dtype=jnp.int32)[None, :]).astype(jnp.int32)
    slot = jnp.sum(picks * (jnp.cumsum(picks, axis=0) - 1), axis=1)
    send_ids = jnp.full((owners, capacity), own_blocks, jnp.int32).at[target, slot].set(owned_index)
    send_pairs = (
        jnp.zeros((owners, capacity), jnp.int32).at[target, slot].set(sensor_of * layers + layer_of)
    )
    wanted_ids, wanted_pairs = (
        lax.all_to_all(send_ids, "gy", split_axis=0, concat_axis=0, tiled=True),
        lax.all_to_all(send_pairs, "gy", split_axis=0, concat_axis=0, tiled=True),
    )
    slot_source = (
        jnp.full((owners, capacity), requests, jnp.int32).at[target, slot].set(request_num)
    )
    landing = (
        wanted_ids.reshape(-1)[None, :] == jnp.arange(own_blocks, dtype=jnp.int32)[:, None]
    ).astype(jnp.float32)
    solution = jnp.zeros_like(right_side)
    residual = right_side
    precond_res = jacobi_inverse * residual

    def global_sum(local_value):
        return lax.psum(local_value, ("gx", "gy"))

    direction = precond_res
    rho_now = global_sum(jnp.sum(residual * precond_res))
    for step in range(ITERS):
        synthesize_padded = with_rim(direction)
        along_rows = jnp.einsum("lab,ac->lcb", synthesize_padded, synth_rows, precision=highest)
        blocks = (
            jnp.einsum("lab,bc->lac", along_rows, synth_cols, precision=highest)
            .reshape(layers, rows_blocks, block_rows, cols_blocks, block_cols)
            .transpose(0, 1, 3, 2, 4)
            .reshape(own_blocks, block_rows, block_cols)
        )
        outgoing = jnp.take(blocks, wanted_ids, axis=0, mode="fill", fill_value=0.0)
        arrived = lax.all_to_all(outgoing, "gy", split_axis=0, concat_axis=0, tiled=True)
        seen = arrived[target, slot].reshape(
            sensors, rows_blocks * cols_blocks, layers, block_rows, block_cols
        )
        slopes = jnp.einsum("sklxy,slyz->skxz", seen, interaction, precision=highest)
        back = jnp.einsum("skxz,slyz->sklxy", slopes, interaction, precision=highest).reshape(
            requests, block_rows, block_cols
        )
        returning = jnp.take(back, slot_source, axis=0, mode="fill", fill_value=0.0)
        landed = lax.all_to_all(returning, "gy", split_axis=0, concat_axis=0, tiled=True)
        summed = jnp.dot(
            landing, landed.reshape(owners * capacity, block_rows * block_cols), precision=highest
        )
        padded = with_rim(
            summed.reshape(layers, rows_blocks, cols_blocks, block_rows, block_cols)
            .transpose(0, 1, 3, 2, 4)
            .reshape(layers, tile_rows, tile_cols)
        )
        along_cols = jnp.einsum("lab,bc->lac", padded, analysis_cols, precision=highest)
        image = (
            jnp.einsum("lab,ac->lcb", along_cols, analysis_rows, precision=highest)
            + prior_weight * direction
        )
        step_size = rho_now / global_sum(jnp.sum(direction * image))
        solution = solution + step_size * direction
        residual = residual - step_size * image
        if step + 1 < ITERS:
            precond_res = jacobi_inverse * residual
            rho_next = global_sum(jnp.sum(residual * precond_res))
            direction = precond_res + rho_next / rho_now * direction
            rho_now = rho_next
    return (solution, residual)


def solution(mesh):
    return jax.shard_map(
        shards,
        mesh=mesh,
        in_specs=(
            P(None, "gx", "gy"),
            P(None, "gx", "gy"),
            P(None, "gx", "gy"),
            P(),
            P(None, "gx", "gy", None),
        ),
        out_specs=(P(None, "gx", "gy"), P(None, "gx", "gy")),
        check_vma=False,
    )
```

profile of v0, /device:TPU:0, one launch (start us, length us, event | category | flops | bytes accessed | tf_op | source)
XLA Modules:
  0.0 1154.9 jit_solution(17234243243100346092)
XLA Ops:
  3.4 10.1 scatter_fusion
  13.5 7.3 all-to-all-start
  33.4 3.9 collective-permute-start.2
  38.8 4.2 collective-permute-done.3
  56.5 5.7 all-to-all-start.1
  65.8 48.2 %all-to-all-done.1 = f32[8,9,64,128]{3,2,1,0:T(8,128)} async-done(((f32[8,9,64,128]{3,2,1,0:T(8,128)}), f32[8,9,64,128]{3,2,1,0:T(8,128)}, u32[]{:S(2)}, u32[]{:S(2)}) %all-to-all-start.1) | async-done | bytes 2359328 | tf_op jit(solution)/shard_map/all_to_all | solution.py:124
  124.3 3.7 gather_fusion.5
  131.4 7.1 all-to-all-start.2
  139.8 54.4 %all-to-all-done.2 = f32[8,9,64,128]{3,2,1,0:T(8,128)} async-done(((f32[8,9,64,128]{3,2,1,0:T(8,128)}), f32[8,9,64,128]{3,2,1,0:T(8,128)}, u32[]{:S(2)}, u32[]{:S(2)}) %all-to-all-start.2) | async-done | bytes 2359328 | tf_op jit(solution)/shard_map/all_to_all | solution.py:133
  213.3 4.5 collective-permute-start.6
  220.8 3.8 fusion.18
  224.6 4.6 multiply_reduce_fusion.6
  229.2 41.6 %all-reduce = (f32[]{:T(128)}, f32[]{:T(128)}) all-reduce(f32[]{:T(128)} %get-tuple-element.7, f32[]{:T(128)} %get-tuple-element.6), channel_id=1, replica_groups=mesh['gx'=4,'gy'=8] {'gx','gy'}, use_global_device_ids=true, to_apply=%region_1.2 | all-reduce | flops 2 | bytes 16 | tf_op jit(solution)/shard_map/psum | solution.py:110
  272.0 4.0 multiply_reduce_fusion.5
  276.0 40.2 %psum.58 = f32[]{:T(128)} all-reduce(f32[]{:T(128)} %get-tuple-element.16), channel_id=1, replica_groups=mesh['gx'=4,'gy'=8] {'gx','gy'}, use_global_device_ids=true, to_apply=%region_9.12 | all-reduce | flops 1 | bytes 8 | tf_op jit(solution)/shard_map/psum | solution.py:110
  321.8 4.8 collective-permute-done.9
  331.4 4.6 collective-permute-done.11
  338.3 3.8 fusion.199
  352.4 57.1 %all_to_all.52 = f32[8,9,64,128]{3,2,1,0:T(8,128)} all-to-all(f32[8,9,64,128]{3,2,1,0:T(8,128)S(1)} %broadcast_select_fusion.5), channel_id=1, replica_groups=mesh['gx'=4,'gy'=8] {'gy'}, dimensions={0} | all-to-all | bytes 4718592 | tf_op jit(solution)/shard_map/all_to_all | solution.py:124
  409.5 3.7 gather_fusion.1
  425.5 59.7 %all_to_all.53 = f32[8,9,64,128]{3,2,1,0:T(8,128)S(1)} all-to-all(f32[8,9,64,128]{3,2,1,0:T(8,128)S(1)} %broadcast_select_fusion.4), channel_id=1, replica_groups=mesh['gx'=4,'gy'=8] {'gy'}, dimensions={0} | all-to-all | bytes 4718592 | tf_op jit(solution)/shard_map/all_to_all | solution.py:133
  509.4 4.0 collective-permute-done.15
  514.4 3.8 fusion.38
  518.2 4.5 multiply_reduce_fusion.4
  522.7 40.1 %psum.59 = f32[]{:T(128)} all-reduce(f32[]{:T(128)} %get-tuple-element.57), channel_id=1, replica_groups=mesh['gx'=4,'gy'=8] {'gx','gy'}, use_global_device_ids=true, to_apply=%region_11.14 | all-reduce | flops 1 | bytes 8 | tf_op jit(solution)/shard_map/psum | solution.py:110
  564.2 4.1 multiply_reduce_fusion.3
  568.3 40.2 %psum.60 = f32[]{:T(128)} all-reduce(f32[]{:T(128)} %get-tuple-element.13), channel_id=1, replica_groups=mesh['gx'=4,'gy'=8] {'gx','gy'}, use_global_device_ids=true, to_apply=%region_13.16 | all-reduce | flops 1 | bytes 8 | tf_op jit(solution)/shard_map/psum | solution.py:110
  614.2 4.8 collective-permute-done.17
  619.1 3.7 collective-permute-start.18
  624.4 4.2 collective-permute-done.19
  631.0 3.8 fusion.196
  645.0 56.2 %all_to_all.54 = f32[8,9,64,128]{3,2,1,0:T(8,128)} all-to-all(f32[8,9,64,128]{3,2,1,0:T(8,128)S(1)} %broadcast_select_fusion.3), channel_id=1, replica_groups=mesh['gx'=4,'gy'=8] {'gy'}, dimensions={0} | all-to-all | bytes 4718592 | tf_op jit(solution)/shard_map/all_to_all | solution.py:124
  717.1 60.0 %all_to_all.55 = f32[8,9,64,128]{3,2,1,0:T(8,128)S(1)} all-to-all(f32[8,9,64,128]{3,2,1,0:T(8,128)S(1)} %broadcast_select_fusion.2), channel_id=1, replica_groups=mesh['gx'=4,'gy'=8] {'gy'}, dimensions={0} | all-to-all | bytes 4718592 | tf_op jit(solution)/shard_map/all_to_all | solution.py:133
  801.3 4.0 collective-permute-done.23
  806.4 3.9 fusion.58
  810.3 4.5 multiply_reduce_fusion.2
  814.8 40.2 %psum.61 = f32[]{:T(128)} all-reduce(f32[]{:T(128)} %get-tuple-element.59), channel_id=1, replica_groups=mesh['gx'=4,'gy'=8] {'gx','gy'}, use_global_device_ids=true, to_apply=%region_15.18 | all-reduce | flops 1 | bytes 8 | tf_op jit(solution)/shard_map/psum | solution.py:110
  856.3 4.1 multiply_reduce_fusion.1
  860.4 40.1 %psum.62 = f32[]{:T(128)} all-reduce(f32[]{:T(128)} %get-tuple-element.10), channel_id=1, replica_groups=mesh['gx'=4,'gy'=8] {'gx','gy'}, use_global_device_ids=true, to_apply=%region_17.20 | all-reduce | flops 1 | bytes 8 | tf_op jit(solution)/shard_map/psum | solution.py:110
  906.5 4.8 collective-permute-done.25
  916.6 4.2 collective-permute-done.27
  923.2 3.8 fusion.193
  937.3 56.3 %all_to_all.56 = f32[8,9,64,128]{3,2,1,0:T(8,128)} all-to-all(f32[8,9,64,128]{3,2,1,0:T(8,128)S(1)} %broadcast_select_fusion.1), channel_id=1, replica_groups=mesh['gx'=4,'gy'=8] {'gy'}, dimensions={0} | all-to-all | bytes 4718592 | tf_op jit(solution)/shard_map/all_to_all | solution.py:124
  1009.5 59.9 %all_to_all.57 = f32[8,9,64,128]{3,2,1,0:T(8,128)S(1)} all-to-all(f32[8,9,64,128]{3,2,1,0:T(8,128)S(1)} %broadcast_select_fusion), channel_id=1, replica_groups=mesh['gx'=4,'gy'=8] {'gy'}, dimensions={0} | all-to-all | bytes 4718592 | tf_op jit(solution)/shard_map/all_to_all | solution.py:133
  1093.7 3.9 collective-permute-done.31
  1098.7 3.9 fusion.78
  1102.6 4.5 multiply_reduce_fusion
  1107.1 40.2 %psum.63 = f32[]{:T(128)} all-reduce(f32[]{:T(128)} %get-tuple-element.61), channel_id=1, replica_groups=mesh['gx'=4,'gy'=8] {'gx','gy'}, use_global_device_ids=true, to_apply=%region_19.22 | all-reduce | flops 1 | bytes 8 | tf_op jit(solution)/shard_map/psum | solution.py:110
  (225 shorter events, 259.1 us)
Async XLA Ops:
  0.6 117.1 %copy-start = (f32[2,4,128,128]{3,2,1,0:T(8,128)S(1)}, f32[2,4,128,128]{3,2,1,0:T(8,128)}, u32[]{:S(2)}) copy-start(f32[2,4,128,128]{3,2,1,0:T(8,128)} %param.12) | copy-start | bytes 1572868
  0.6 20.1 %copy-start.15 = (f32[4,256,256]{2,1,0:T(8,128)S(1)}, f32[4,256,256]{2,1,0:T(8,128)}, u32[]{:S(2)}) copy-start(f32[4,256,256]{2,1,0:T(8,128)} %param.11) | copy-start | bytes 3145732
  13.5 15.8 %all-to-all-start = ((s32[8,1,9]{2,1,0:T(1,128)}), s32[8,1,9]{2,1,0:T(1,128)S(1)}, u32[]{:S(2)}, u32[]{:S(2)}) async-start(s32[8,1,9]{2,1,0:T(1,128)} %bitcast.4), calls=%async_computation | async-start | bytes 8192 | tf_op jit(solution)/shard_map/all_to_all | solution.py:96
  21.1 4.3 copy-start.9
  26.5 3.2 collective-permute-start
  27.9 5.3 collective-permute-start.1
  33.4 5.4 collective-permute-start.2
  37.3 5.7 collective-permute-start.3
  56.5 57.4 %all-to-all-start.1 = ((f32[8,9,64,128]{3,2,1,0:T(8,128)}), f32[8,9,64,128]{3,2,1,0:T(8,128)}, u32[]{:S(2)}, u32[]{:S(2)}) async-start(f32[8,9,64,128]{3,2,1,0:T(8,128)} %broadcast_select_fusion.7), calls=%async_computation.1 | async-start | bytes 4718592 | tf_op jit(solution)/shard_map/all_to_all | solution.py:124
  131.4 62.8 %all-to-all-start.2 = ((f32[8,9,64,128]{3,2,1,0:T(8,128)}), f32[8,9,64,128]{3,2,1,0:T(8,128)}, u32[]{:S(2)}, u32[]{:S(2)}) async-start(f32[8,9,64,128]{3,2,1,0:T(8,128)} %broadcast_select_fusion.6), calls=%async_computation.2 | async-start | bytes 4718592 | tf_op jit(solution)/shard_map/all_to_all | solution.py:133
  204.2 6.3 copy-start.11
  204.2 3.6 collective-permute-start.4
  206.2 3.1 collective-permute-start.5
  212.0 7.7 collective-permute-start.7
  213.3 6.1 collective-permute-start.6
  219.5 5.1 copy-start.3
  220.8 3.8 copy-start.10
  319.0 2.8 collective-permute-start.8
  320.3 6.3 collective-permute-start.9
  326.7 4.7 collective-permute-start.10
  329.6 6.3 collective-permute-start.11
  495.3 3.3 collective-permute-start.12
  497.3 3.1 collective-permute-start.13
  504.0 5.1 collective-permute-start.14
  507.6 5.7 collective-permute-start.15
  514.4 3.8 copy-start.4
  611.2 17.4 %copy-start.1 = (f32[4,256,256]{1,2,0:T(8,128)}, f32[4,256,256]{1,2,0:T(8,128)S(1)}, u32[]{:S(2)}) copy-start(f32[4,256,256]{1,2,0:T(8,128)S(1)} %multiply_add_fusion.2) | copy-start | bytes 3145732
  611.4 2.8 collective-permute-start.16
  612.7 6.3 collective-permute-start.17
  619.1 5.3 collective-permute-start.18
  622.9 5.7 collective-permute-start.19
  787.2 3.3 collective-permute-start.20
  789.3 3.1 collective-permute-start.21
  796.0 5.1 collective-permute-start.22
  799.6 5.7 collective-permute-start.23
  806.4 3.9 copy-start.2
  806.4 3.9 copy-start.5
  903.5 17.3 %copy-start.7 = (f32[4,256,256]{1,2,0:T(8,128)}, f32[4,256,256]{1,2,0:T(8,128)S(1)}, u32[]{:S(2)}) copy-start(f32[4,256,256]{1,2,0:T(8,128)S(1)} %multiply_add_fusion.1) | copy-start | bytes 3145732
  903.7 2.8 collective-permute-start.24
  905.0 6.3 collective-permute-start.25
  911.4 5.2 collective-permute-start.26
  915.1 5.7 collective-permute-start.27
  1079.5 3.3 collective-permute-start.28
  1081.6 3.1 collective-permute-start.29
  1088.3 5.2 collective-permute-start.30
  1091.9 5.7 collective-permute-start.31
  1098.7 3.9 copy-start.6
  1098.7 3.9 copy-start.8
  (3 other events, 7.4 us)
where the time goes:
time: 1170 us; the launch traced here: 1150 us
  blocking collectives  632 us (54%)
  waiting for transfers between devices  157 us (13%)
  local copies, waits for them, and re-layouts  131 us (11%)
  matrix products  94.2 us (8%)
  starting transfers between devices  84.8 us (7%)
  other arithmetic  44.8 us (4%)
    psum x7, blocking collectives, global_sum(): return lax.psum(local_value, ('gx', 'gy'))  283 us
    all_to_all x3, blocking collectives, shards(): lax.all_to_all(returning, 'gy', split_axis=0, concat_axis=0, tiled=True)  180 us
    all_to_all x3, blocking collectives, shards(): lax.all_to_all(outgoing, 'gy', split_axis=0, concat_axis=0, tiled=True)  170 us
    all_to_all x1, waiting for transfers between devices, shards(): lax.all_to_all(returning, 'gy', split_axis=0, concat_axis=0, tiled=True)  54.4 us
    ppermute x16, waiting for transfers between devices, extended(): lax.ppermute(lax.slice_in_dim(block, 0, width, axis=dim), axis, backward)  53.8 us
    all_to_all x1, waiting for transfers between devices, shards(): lax.all_to_all(outgoing, 'gy', split_axis=0, concat_axis=0, tiled=True)  48.2 us
    ppermute x16, starting transfers between devices, extended(): lax.ppermute(lax.slice_in_dim(block, block.shape[dim] - width, None, axis...  42.3 us
  transfers between devices with their start and end apart: 35, of which 22 were waited for; matrix products, arithmetic and copies ran while one was open for 1% of the time, Pallas kernels for 0%

commit v1 on v0

--- a/solution.py
+++ b/solution.py
@@ -107,7 +107,7 @@
     precond_res = jacobi_inverse * residual
 
     def global_sum(local_value):
-        return lax.psum(local_value, ("gx", "gy"))
+        return lax.psum(lax.psum(local_value, "gy"), "gx")
 
     direction = precond_res
     rho_now = global_sum(jnp.sum(residual * precond_res))

time: 1170 us -> 1060 us (0.906)
  blocking collectives: 632 us -> 526 us
    psum x7 -> x14, blocking collectives: 283 us -> 178 us  [global_sum(): return lax.psum(lax.psum(local_value, 'gy'), 'gx')]
where the time goes in v1:
time: 1060 us; the launch traced here: 1050 us
  blocking collectives  526 us (50%)
  waiting for transfers between devices  154 us (15%)
  local copies, waits for them, and re-layouts  131 us (12%)
  matrix products  94.2 us (9%)
  starting transfers between devices  88 us (8%)
  other arithmetic  44.8 us (4%)
  between operations  10.8 us (1%)
    all_to_all x3, blocking collectives, shards(): lax.all_to_all(returning, 'gy', split_axis=0, concat_axis=0, tiled=True)  179 us
    psum x14, blocking collectives, global_sum(): return lax.psum(lax.psum(local_value, 'gy'), 'gx')  178 us
    all_to_all x3, blocking collectives, shards(): lax.all_to_all(outgoing, 'gy', split_axis=0, concat_axis=0, tiled=True)  168 us
    all_to_all x1, waiting for transfers between devices, shards(): lax.all_to_all(returning, 'gy', split_axis=0, concat_axis=0, tiled=True)  54.3 us
    ppermute x16, waiting for transfers between devices, extended(): lax.ppermute(lax.slice_in_dim(block, 0, width, axis=dim), axis, backward)  50.4 us
    all_to_all x1, waiting for transfers between devices, shards(): lax.all_to_all(outgoing, 'gy', split_axis=0, concat_axis=0, tiled=True)  48.2 us
    ppermute x16, starting transfers between devices, extended(): lax.ppermute(lax.slice_in_dim(block, block.shape[dim] - width, None, axis...  45.6 us
    ppermute x16, starting transfers between devices, extended(): lax.ppermute(lax.slice_in_dim(block, 0, width, axis=dim), axis, backward)  22.2 us
  transfers between devices with their start and end apart: 35, of which 22 were waited for; matrix products, arithmetic and copies ran while one was open for 1% of the time, Pallas kernels for 0%

profile of v1, /device:TPU:0, one launch (start us, length us, event | category | flops | bytes accessed | tf_op | source)
XLA Modules:
  0.0 1047.8 jit_solution(9646645353159933572)
XLA Ops:
  3.4 10.2 scatter_fusion
  13.6 7.3 all-to-all-start
  33.5 3.9 collective-permute-start.2
  38.9 4.2 collective-permute-done.3
  56.6 5.8 all-to-all-start.1
  66.0 48.2 %all-to-all-done.1 = f32[8,9,64,128]{3,2,1,0:T(8,128)} async-done(((f32[8,9,64,128]{3,2,1,0:T(8,128)}), f32[8,9,64,128]{3,2,1,0:T(8,128)}, u32[]{:S(2)}, u32[]{:S(2)}) %all-to-all-start.1) | async-done | bytes 2359328 | tf_op jit(solution)/shard_map/all_to_all | solution.py:124
  131.5 7.1 all-to-all-start.2
  140.0 54.3 %all-to-all-done.2 = f32[8,9,64,128]{3,2,1,0:T(8,128)} async-done(((f32[8,9,64,128]{3,2,1,0:T(8,128)}), f32[8,9,64,128]{3,2,1,0:T(8,128)}, u32[]{:S(2)}, u32[]{:S(2)}) %all-to-all-start.2) | async-done | bytes 2359328 | tf_op jit(solution)/shard_map/all_to_all | solution.py:133
  213.4 4.5 collective-permute-start.6
  220.9 3.8 fusion.18
  224.7 4.5 multiply_reduce_fusion.6
  229.3 21.4 %all-reduce = (f32[]{:T(128)}, f32[]{:T(128)}) all-reduce(f32[]{:T(128)} %get-tuple-element.7, f32[]{:T(128)} %get-tuple-element.6), channel_id=1, replica_groups=mesh['gx'=4,'gy'=8] {'gy'}, use_global_device_ids=true, to_apply=%region_1.2 | all-reduce | flops 2 | bytes 16 | tf_op jit(solution)/shard_map/psum | solution.py:110
  250.7 6.3 all-reduce.1
  258.4 4.0 multiply_reduce_fusion.5
  262.4 17.8 %psum.116 = f32[]{:T(128)} all-reduce(f32[]{:T(128)} %get-tuple-element.18), channel_id=1, replica_groups=mesh['gx'=4,'gy'=8] {'gy'}, use_global_device_ids=true, to_apply=%region_11.14 | all-reduce | flops 1 | bytes 8 | tf_op jit(solution)/shard_map/psum | solution.py:110
  280.1 6.3 psum.117
  296.8 3.9 collective-permute-start.10
  302.2 4.2 collective-permute-done.11
  322.9 56.1 %all_to_all.52 = f32[8,9,64,128]{3,2,1,0:T(8,128)} all-to-all(f32[8,9,64,128]{3,2,1,0:T(8,128)S(1)} %broadcast_select_fusion.5), channel_id=1, replica_groups=mesh['gx'=4,'gy'=8] {'gy'}, dimensions={0} | all-to-all | bytes 4718592 | tf_op jit(solution)/shard_map/all_to_all | solution.py:124
  394.9 59.8 %all_to_all.53 = f32[8,9,64,128]{3,2,1,0:T(8,128)S(1)} all-to-all(f32[8,9,64,128]{3,2,1,0:T(8,128)S(1)} %broadcast_select_fusion.4), channel_id=1, replica_groups=mesh['gx'=4,'gy'=8] {'gy'}, dimensions={0} | all-to-all | bytes 4718592 | tf_op jit(solution)/shard_map/all_to_all | solution.py:133
  478.6 4.2 collective-permute-done.15
  483.8 3.8 fusion.38
  487.7 4.5 multiply_reduce_fusion.4
  492.2 19.4 %psum.118 = f32[]{:T(128)} all-reduce(f32[]{:T(128)} %get-tuple-element.59), channel_id=1, replica_groups=mesh['gx'=4,'gy'=8] {'gy'}, use_global_device_ids=true, to_apply=%region_14.17 | all-reduce | flops 1 | bytes 8 | tf_op jit(solution)/shard_map/psum | solution.py:110
  511.6 6.3 psum.119
  519.2 4.0 multiply_reduce_fusion.3
  523.2 18.1 %psum.120 = f32[]{:T(128)} all-reduce(f32[]{:T(128)} %get-tuple-element.15), channel_id=1, replica_groups=mesh['gx'=4,'gy'=8] {'gy'}, use_global_device_ids=true, to_apply=%region_17.20 | all-reduce | flops 1 | bytes 8 | tf_op jit(solution)/shard_map/psum | solution.py:110
  541.3 6.3 psum.121
  563.4 3.9 collective-permute-done.19
  583.8 56.1 %all_to_all.54 = f32[8,9,64,128]{3,2,1,0:T(8,128)} all-to-all(f32[8,9,64,128]{3,2,1,0:T(8,128)S(1)} %broadcast_select_fusion.3), channel_id=1, replica_groups=mesh['gx'=4,'gy'=8] {'gy'}, dimensions={0} | all-to-all | bytes 4718592 | tf_op jit(solution)/shard_map/all_to_all | solution.py:124
  655.8 59.7 %all_to_all.55 = f32[8,9,64,128]{3,2,1,0:T(8,128)S(1)} all-to-all(f32[8,9,64,128]{3,2,1,0:T(8,128)S(1)} %broadcast_select_fusion.2), channel_id=1, replica_groups=mesh['gx'=4,'gy'=8] {'gy'}, dimensions={0} | all-to-all | bytes 4718592 | tf_op jit(solution)/shard_map/all_to_all | solution.py:133
  739.5 4.2 collective-permute-done.23
  744.7 3.9 fusion.58
  748.7 4.5 multiply_reduce_fusion.2
  753.2 19.4 %psum.122 = f32[]{:T(128)} all-reduce(f32[]{:T(128)} %get-tuple-element.61), channel_id=1, replica_groups=mesh['gx'=4,'gy'=8] {'gy'}, use_global_device_ids=true, to_apply=%region_20.23 | all-reduce | flops 1 | bytes 8 | tf_op jit(solution)/shard_map/psum | solution.py:110
  772.6 6.3 psum.123
  780.1 4.1 multiply_reduce_fusion.1
  784.2 18.2 %psum.124 = f32[]{:T(128)} all-reduce(f32[]{:T(128)} %get-tuple-element.12), channel_id=1, replica_groups=mesh['gx'=4,'gy'=8] {'gy'}, use_global_device_ids=true, to_apply=%region_23.26 | all-reduce | flops 1 | bytes 8 | tf_op jit(solution)/shard_map/psum | solution.py:110
  802.3 6.3 psum.125
  824.5 4.2 collective-permute-done.27
  831.1 3.8 fusion.193
  845.2 56.1 %all_to_all.56 = f32[8,9,64,128]{3,2,1,0:T(8,128)} all-to-all(f32[8,9,64,128]{3,2,1,0:T(8,128)S(1)} %broadcast_select_fusion.1), channel_id=1, replica_groups=mesh['gx'=4,'gy'=8] {'gy'}, dimensions={0} | all-to-all | bytes 4718592 | tf_op jit(solution)/shard_map/all_to_all | solution.py:124
  917.2 59.9 %all_to_all.57 = f32[8,9,64,128]{3,2,1,0:T(8,128)S(1)} all-to-all(f32[8,9,64,128]{3,2,1,0:T(8,128)S(1)} %broadcast_select_fusion), channel_id=1, replica_groups=mesh['gx'=4,'gy'=8] {'gy'}, dimensions={0} | all-to-all | bytes 4718592 | tf_op jit(solution)/shard_map/all_to_all | solution.py:133
  1001.4 4.0 collective-permute-done.31
  1006.5 3.9 fusion.78
  1010.4 4.5 multiply_reduce_fusion
  1014.9 19.4 %psum.126 = f32[]{:T(128)} all-reduce(f32[]{:T(128)} %get-tuple-element.63), channel_id=1, replica_groups=mesh['gx'=4,'gy'=8] {'gy'}, use_global_device_ids=true, to_apply=%region_26.29 | all-reduce | flops 1 | bytes 8 | tf_op jit(solution)/shard_map/psum | solution.py:110
  1034.3 6.3 psum.127
  (232 shorter events, 287.9 us)
Async XLA Ops:
  0.6 117.2 %copy-start = (f32[2,4,128,128]{3,2,1,0:T(8,128)S(1)}, f32[2,4,128,128]{3,2,1,0:T(8,128)}, u32[]{:S(2)}) copy-start(f32[2,4,128,128]{3,2,1,0:T(8,128)} %param.12) | copy-start | bytes 1572868
  0.6 20.2 %copy-start.15 = (f32[4,256,256]{2,1,0:T(8,128)S(1)}, f32[4,256,256]{2,1,0:T(8,128)}, u32[]{:S(2)}) copy-start(f32[4,256,256]{2,1,0:T(8,128)} %param.11) | copy-start | bytes 3145732
  13.6 15.8 %all-to-all-start = ((s32[8,1,9]{2,1,0:T(1,128)}), s32[8,1,9]{2,1,0:T(1,128)S(1)}, u32[]{:S(2)}, u32[]{:S(2)}) async-start(s32[8,1,9]{2,1,0:T(1,128)} %bitcast.4), calls=%async_computation | async-start | bytes 8192 | tf_op jit(solution)/shard_map/all_to_all | solution.py:96
  21.2 4.3 copy-start.9
  26.6 3.2 collective-permute-start
  28.1 5.3 collective-permute-start.1
  33.5 5.4 collective-permute-start.2
  37.4 5.7 collective-permute-start.3
  56.6 57.6 %all-to-all-start.1 = ((f32[8,9,64,128]{3,2,1,0:T(8,128)}), f32[8,9,64,128]{3,2,1,0:T(8,128)}, u32[]{:S(2)}, u32[]{:S(2)}) async-start(f32[8,9,64,128]{3,2,1,0:T(8,128)} %broadcast_select_fusion.7), calls=%async_computation.1 | async-start | bytes 4718592 | tf_op jit(solution)/shard_map/all_to_all | solution.py:124
  131.5 62.8 %all-to-all-start.2 = ((f32[8,9,64,128]{3,2,1,0:T(8,128)}), f32[8,9,64,128]{3,2,1,0:T(8,128)}, u32[]{:S(2)}, u32[]{:S(2)}) async-start(f32[8,9,64,128]{3,2,1,0:T(8,128)} %broadcast_select_fusion.6), calls=%async_computation.2 | async-start | bytes 4718592 | tf_op jit(solution)/shard_map/all_to_all | solution.py:133
  204.3 6.3 copy-start.11
  204.3 3.9 collective-permute-start.4
  206.3 3.1 collective-permute-start.5
  212.1 7.7 collective-permute-start.7
  213.4 6.1 collective-permute-start.6
  219.6 5.1 copy-start.3
  220.9 3.8 copy-start.10
  289.2 3.7 collective-permute-start.8
  291.4 5.3 collective-permute-start.9
  296.8 5.4 collective-permute-start.10
  300.7 5.7 collective-permute-start.11
  464.7 3.3 collective-permute-start.12
  466.7 3.1 collective-permute-start.13
  473.5 4.9 collective-permute-start.14
  477.1 5.7 collective-permute-start.15
  483.8 3.8 copy-start.4
  550.3 17.1 %copy-start.1 = (f32[4,256,256]{1,2,0:T(8,128)}, f32[4,256,256]{1,2,0:T(8,128)S(1)}, u32[]{:S(2)}) copy-start(f32[4,256,256]{1,2,0:T(8,128)S(1)} %multiply_add_fusion.2) | copy-start | bytes 3145732
  550.5 3.7 collective-permute-start.16
  552.7 5.3 collective-permute-start.17
  558.1 5.3 collective-permute-start.18
  561.6 5.7 collective-permute-start.19
  725.6 3.3 collective-permute-start.20
  727.6 3.1 collective-permute-start.21
  734.4 4.9 collective-permute-start.22
  738.0 5.7 collective-permute-start.23
  744.7 3.9 copy-start.2
  744.7 3.9 copy-start.5
  811.7 17.1 %copy-start.7 = (f32[4,256,256]{1,2,0:T(8,128)}, f32[4,256,256]{1,2,0:T(8,128)S(1)}, u32[]{:S(2)}) copy-start(f32[4,256,256]{1,2,0:T(8,128)S(1)} %multiply_add_fusion.1) | copy-start | bytes 3145732
  811.9 3.7 collective-permute-start.24
  814.1 5.3 collective-permute-start.25
  819.4 5.1 collective-permute-start.26
  823.0 5.7 collective-permute-start.27
  987.3 3.3 collective-permute-start.28
  989.3 3.1 collective-permute-start.29
  996.1 5.1 collective-permute-start.30
  999.7 5.7 collective-permute-start.31
  1006.5 3.9 copy-start.6
  1006.5 3.9 copy-start.8
  (3 other events, 7.4 us)
